TPU v7x, 256 devices: a whole 4x4x8 slice. The times are simulated.
256 devices in a mesh: dp: 4 (over x_lo, core), expert: 64 (over z, y, x_hi).
Axes of the slice: x: 4 (x_hi: 2, x_lo: 2; x = x_hi * 2 + x_lo), y: 4, z: 8, core: 2. Of those that a mesh axis runs over, the one named last changes fastest.
Arguments:
- prev_acts: bfloat16 [4, 64, 128, 3584], P('dp', 'expert'), may hold values from -6 to 6
- prev_cot: bfloat16 [4, 64, 128, 512], P('dp', 'expert'), may hold values from -0.59765625 to 0.59765625
- weights: bfloat16 [64, 3584, 512], P('expert', 'dp'), may hold values from -0.09375 to 0.09375
- first_moment: float32 [64, 3584, 512], P('expert', 'dp'), may hold values from -1.8 to 1.8
- second_moment: float32 [64, 3584, 512], P('expert', 'dp'), may hold values from 0.1 to 2
- tokens: bfloat16 [4, 64, 128, 3584], P('dp', 'expert'), may hold values from -6 to 6
- routing: int32 [4, 64, 128, 2], P('dp', 'expert'), may hold values from 0 to 15, all different within a row; in each aligned block of 128 rows (0 to 127, 128 to 255, ..., all dimensions but the last counted through in order) at most 24 rows name the same one
- gates: bfloat16 [4, 64, 128, 2], P('dp', 'expert'), may hold values from 0.19921875 to 1
- token_counts: int32 [4, 64], P('dp', 'expert'), may hold values from 64 to 128
- old_owner: int32 [16], replicated, may hold values from 0 to 15, each once
- new_owner: int32 [16], replicated, may hold values from 0 to 15, each once
Outputs:
- expert_hidden: bfloat16 [4, 64, 1536, 256], P('dp', 'expert')
- new_weights: bfloat16 [64, 3584, 512], P('expert', 'dp')
- new_first: float32 [64, 3584, 512], P('expert', 'dp')
- new_second: float32 [64, 3584, 512], P('expert', 'dp')
Inputs may be any that keep to these rules, and one draw needn't show every extreme that they name: `routing`: each token names 2 different hot experts; within the rows of one device no hot expert is named by more than 24 rows. `old_owner`: each is a permutation of the 16 groups. `new_owner`: each is a permutation of the 16 groups.
All inputs are finite; a program needn't handle non-finite values.
Results may differ from a plain program's by a relative error of at most 0.013.
Values may be sent and summed in bfloat16 or wider, within the bound.
No kernel may reach another device: no remote copies, remote signals or barrier semaphores. Data moves between devices by JAX's collectives and lax.ppermute only.
A program may use at most 128 MiB of HBM per device.

v0:
```python
import jax
import jax.numpy as jnp
from jax import lax
from jax.sharding import PartitionSpec as P

D = 3584
GRP = 4
beta_first = 0.9
beta_second = 0.95
learning = 0.00022
decay_rate = 0.1
epsilon = 1e-08
first_fix = 1.0 - 0.9**40
second_fix = 1.0 - 0.95**40


def adamw(weight_now, first_now, second_now, gradient):
    first_next = beta_first * first_now + (1.0 - beta_first) * gradient
    second_next = beta_second * second_now + (1.0 - beta_second) * gradient * gradient
    stepped = weight_now.astype(jnp.float32) * (1.0 - learning * decay_rate) - learning * (
        first_next / first_fix
    ) / (jnp.sqrt(second_next / second_fix) + epsilon)
    return (stepped.astype(jnp.bfloat16), jnp.stack([first_next, second_next]))


def migrate(weight_now, moment_stack, source, experts):
    rows_dev = weight_now.shape[0]
    width = weight_now.shape[1]
    layers = moment_stack.shape[0]
    piece_rows = rows_dev // experts
    weight_split = weight_now.reshape(experts, piece_rows, width)
    moment_split = moment_stack.reshape(layers, experts, piece_rows, width)
    weight_spread = lax.all_to_all(weight_split, "expert", split_axis=0, concat_axis=0, tiled=True)
    moment_spread = lax.all_to_all(moment_split, "expert", split_axis=1, concat_axis=1, tiled=True)
    weight_sorted = jnp.take(weight_spread, source, axis=0)
    moment_sorted = jnp.take(moment_spread, source, axis=1)
    weight_home = lax.all_to_all(weight_sorted, "expert", split_axis=0, concat_axis=0, tiled=True)
    moment_home = lax.all_to_all(moment_sorted, "expert", split_axis=1, concat_axis=1, tiled=True)
    return (weight_home.reshape(rows_dev, width), moment_home.reshape(layers, rows_dev, width))


def pack_tokens(token_block, route_block, gate_block, limit, hot_count, capacity):
    hot_index = jnp.arange(hot_count, dtype=jnp.int32)
    valid = jnp.arange(token_block.shape[0], dtype=jnp.int32) < limit
    hits = (route_block[:, :, None] == hot_index[None, None, :]) & valid[:, None, None]
    named = jnp.sum(hits.astype(jnp.int32), axis=1)
    scales = jnp.sum(jnp.where(hits, gate_block.astype(jnp.float32)[:, :, None], 0.0), axis=1)
    ranks = jnp.cumsum(named, axis=0) - named
    slots = jnp.arange(capacity, dtype=jnp.int32)
    placed = (ranks.T[:, None, :] == slots[None, :, None]) & (named.T[:, None, :] == 1)
    packed = jnp.einsum(
        "hct,td->hcd", placed.astype(jnp.bfloat16), token_block, preferred_element_type=jnp.float32
    ).astype(jnp.bfloat16)
    gate_scale = jnp.einsum("hct,th->hc", placed.astype(jnp.float32), scales).astype(jnp.bfloat16)
    return (packed, gate_scale)


def local(
    prev_acts,
    prev_cot,
    weights,
    first_moment,
    second_moment,
    tokens,
    routing,
    gates,
    token_counts,
    old_owner,
    new_owner,
):
    experts = lax.axis_size("expert")
    groups = experts // GRP
    token_slots = tokens.shape[2]
    capacity = min(token_slots, 3 * token_slots // groups)
    width = weights.shape[2]
    hidden_units = width // 2
    activations = prev_acts[0, 0]
    cotangent = prev_cot[0, 0]
    hot_index = jnp.arange(groups, dtype=jnp.int32)
    holder = jnp.sum(
        jnp.where(new_owner[None, :] == hot_index[:, None], hot_index[None, :], 0), axis=1
    )
    owners = jnp.arange(experts, dtype=jnp.int32)
    source = jnp.take(old_owner, jnp.take(holder, owners // GRP)) * GRP + owners % GRP
    columns = activations
    grads = lax.psum_scatter(
        lax.dot_general(
            columns, cotangent, (((0,), (0,)), ((), ())), preferred_element_type=jnp.float32
        ).astype(jnp.bfloat16),
        "dp",
        scatter_dimension=0,
        tiled=True,
    ).astype(jnp.float32)
    stepped, moment_stack = adamw(weights[0], first_moment[0], second_moment[0], grads)
    new_weight, moments = migrate(stepped, moment_stack, source, experts)
    packed, gate_scale = pack_tokens(
        tokens[0, 0], routing[0, 0], gates[0, 0], token_counts[0, 0], groups, capacity
    )
    to_group = jnp.take(packed, holder, axis=0)
    scale_group = jnp.take(gate_scale, holder, axis=0)
    scale_send = jnp.repeat(scale_group, GRP, axis=0)
    full_send = jnp.repeat(to_group, GRP, axis=0)
    received, scale_in = (
        lax.all_to_all(full_send, "expert", split_axis=0, concat_axis=0, tiled=True),
        lax.all_to_all(scale_send, "expert", split_axis=0, concat_axis=0, tiled=True),
    )
    token_rows = received.reshape(experts * capacity, D)
    columns = token_rows
    projected = jnp.dot(
        columns,
        lax.all_gather(new_weight, "dp", axis=0, tiled=True),
        preferred_element_type=jnp.float32,
    )
    scaling = scale_in.reshape(experts * capacity).astype(jnp.float32)
    result = (
        jax.nn.silu(projected[:, :hidden_units]) * projected[:, hidden_units:] * scaling[:, None]
    )
    hidden = result.astype(jnp.bfloat16).reshape(1, 1, experts * capacity, hidden_units)
    return (hidden, new_weight[None], moments[0][None], moments[1][None])


def solution(mesh):
    in_specs = (
        P("dp", "expert", None, None),
        P("dp", "expert", None, None),
        P("expert", "dp", None),
        P("expert", "dp", None),
        P("expert", "dp", None),
        P("dp", "expert", None, None),
        P("dp", "expert", None, None),
        P("dp", "expert", None, None),
        P("dp", "expert"),
        P(),
        P(),
    )
    out_specs = (
        P("dp", "expert", None, None),
        P("expert", "dp", None),
        P("expert", "dp", None),
        P("expert", "dp", None),
    )
    return jax.shard_map(local, mesh=mesh, in_specs=in_specs, out_specs=out_specs, check_vma=False)
```

profile of v0, /device:TPU:32, one launch (start us, length us, event | category | flops | bytes accessed | tf_op | source)
XLA Modules:
  0.0 610.4 jit_solution(13180646358381109086)
XLA Ops:
  7.2 1.1 copy-done
  8.4 3.8 convolution_convert_fusion
  13.0 0.1 copy.40
  13.1 0.2 reduce_window_sum.11
  13.4 45.2 %reduce-scatter.2.cloned.1.call-done = bf16[896,512]{1,0:T(8,128)(2,1)} async-done(((bf16[3584,512]{1,0:T(8,128)(2,1)}), bf16[896,512]{1,0:T(8,128)(2,1)}) %reduce-scatter.2.cloned.1.call-update) | async-done | bytes 917520 | tf_op jit(solution)/shard_map/reduce_scatter | solution.py:86
  58.6 5.4 fusion.2
  64.1 1.2 reshape.97
  65.3 12.7 %all-to-all-start.1 = ((bf16[64,14,512]{2,1,0:T(8,128)(2,1)}), bf16[64,14,512]{2,1,0:T(8,128)(2,1)S(1)}, u32[]{:S(2)}, u32[]{:S(2)}) async-start(bf16[64,14,512]{2,1,0:T(8,128)(2,1)} %reshape.97), calls=%async_computation.2 | async-start | bytes 2097152 | tf_op jit(solution)/shard_map/all_to_all | solution.py:33
  78.0 0.2 fusion.9
  78.2 0.1 select_reduce_fusion.1
  78.4 0.6 gather_fusion.2
  79.0 0.1 broadcast_select_fusion.2
  79.0 0.6 copy.43
  79.7 0.8 gather_fusion.4
  80.5 0.8 gather_fusion.5
  81.3 27.3 %all-to-all-done.1 = bf16[64,14,512]{2,1,0:T(8,128)(2,1)S(1)} async-done(((bf16[64,14,512]{2,1,0:T(8,128)(2,1)}), bf16[64,14,512]{2,1,0:T(8,128)(2,1)S(1)}, u32[]{:S(2)}, u32[]{:S(2)}) %all-to-all-start.1) | async-done | bytes 917536 | tf_op jit(solution)/shard_map/all_to_all | solution.py:33
  108.6 6.0 all-to-all-start.3
  114.6 0.6 gather_fusion.1
  115.2 1.1 broadcast_select_fusion.1
  116.3 9.2 %all-to-all-done.3 = bf16[64,1,24]{2,1,0:T(2,128)(2,1)S(1)} async-done(((bf16[64,1,24]{2,1,0:T(2,128)(2,1)}), bf16[64,1,24]{2,1,0:T(2,128)(2,1)S(1)}, u32[]{:S(2)}, u32[]{:S(2)}) %all-to-all-start.3) | async-done | bytes 3104 | tf_op jit(solution)/shard_map/all_to_all | solution.py:105
  125.5 5.6 all-to-all-start.2
  131.1 2.7 stack.10
  133.8 2.7 stack.9
  136.4 2.7 pad_maximum_fusion
  139.2 5.2 copy.44
  144.3 15.2 %all-to-all-done.2 = bf16[64,14,512]{2,1,0:T(8,128)(2,1)S(1)} async-done(((bf16[64,14,512]{2,1,0:T(8,128)(2,1)}), bf16[64,14,512]{2,1,0:T(8,128)(2,1)S(1)}, u32[]{:S(2)}, u32[]{:S(2)}) %all-to-all-start.2) | async-done | bytes 917536 | tf_op jit(solution)/shard_map/all_to_all | solution.py:37
  159.5 6.4 %all-to-all-start.4 = ((f32[2,64,14,512]{3,0,2,1:T(2,128)}), f32[2,64,14,512]{3,0,2,1:T(2,128)}, u32[]{:S(2)}, u32[]{:S(2)}) async-start(f32[2,64,14,512]{3,0,2,1:T(2,128)} %copy.44), calls=%async_computation.5 | async-start | bytes 7340032 | tf_op jit(solution)/shard_map/all_to_all | solution.py:34
  166.0 2.4 convolution_convert_fusion.1
  168.4 4.1 gather_fusion
  172.4 3.7 broadcast_select_fusion
  176.1 73.4 %all-to-all-done.4 = f32[2,64,14,512]{3,0,2,1:T(2,128)} async-done(((f32[2,64,14,512]{3,0,2,1:T(2,128)}), f32[2,64,14,512]{3,0,2,1:T(2,128)}, u32[]{:S(2)}, u32[]{:S(2)}) %all-to-all-start.4) | async-done | bytes 3670048 | tf_op jit(solution)/shard_map/all_to_all | solution.py:34
  249.5 6.6 %broadcast_in_dim.92 = bf16[16,4,24,3584]{3,2,1,0:T(8,128)(2,1)} broadcast(bf16[16,24,3584]{2,1,0:T(8,128)(2,1)} %broadcast_select_fusion), dimensions={0,2,3} | broadcast | bytes 13762560 | tf_op jit(solution)/shard_map/broadcast_in_dim | solution.py:102
  256.1 7.1 %all-to-all-start = ((bf16[64,24,3584]{2,1,0:T(8,128)(2,1)}), bf16[64,24,3584]{2,1,0:T(8,128)(2,1)}, u32[]{:S(2)}, u32[]{:S(2)}) async-start(bf16[64,24,3584]{2,1,0:T(8,128)(2,1)} %bitcast.52), calls=%async_computation | async-start | bytes 22020096 | tf_op jit(solution)/shard_map/all_to_all | solution.py:104
  263.2 1.2 reshape.98
  264.4 8.1 %gather_fusion.3 = f32[64,2,14,512]{3,1,2,0:T(2,128)} fusion(f32[2,64,14,512]{3,0,2,1:T(2,128)} %all-to-all-done.4, s32[1024]{0:T(1024)S(1)} %pad_clamp_fusion), kind=kCustom, calls=%fused_computation.5 | custom fusion | bytes 7340288 | tf_op jit(solution)/shard_map/jit(_take)/gather | solution.py:36
  272.5 5.8 select_bitcast_fusion
  278.3 224.6 %all-to-all-done = bf16[64,24,3584]{2,1,0:T(8,128)(2,1)} async-done(((bf16[64,24,3584]{2,1,0:T(8,128)(2,1)}), bf16[64,24,3584]{2,1,0:T(8,128)(2,1)}, u32[]{:S(2)}, u32[]{:S(2)}) %all-to-all-start) | async-done | bytes 11010080 | tf_op jit(solution)/shard_map/all_to_all | solution.py:104
  502.9 9.1 %all-to-all-start.5 = ((f32[2,64,14,512]{3,0,2,1:T(2,128)}), f32[2,64,14,512]{3,0,2,1:T(2,128)}, u32[]{:S(2)}, u32[]{:S(2)}) async-start(f32[2,64,14,512]{3,0,2,1:T(2,128)} %select_bitcast_fusion), calls=%async_computation.6 | async-start | bytes 7340032 | tf_op jit(solution)/shard_map/all_to_all | solution.py:38
  512.1 0.1 convert_reduce_fusion
  512.2 0.1 reshape.101
  512.2 1.2 broadcast_in_dim_reshape.3
  513.4 9.7 %fusion.23 = f32[1536,512]{1,0:T(8,128)S(1)} fusion(bf16[1536,3584]{1,0:T(8,128)(2,1)} %bitcast.9, bf16[3584,512]{1,0:T(8,128)(2,1)} %all-gather.2.cloned.1.call-done), kind=kOutput, calls=%fused_computation.65 | convolution fusion | flops 5637144576 | bytes 17825792 | tf_op jit(solution)/shard_map/dot_general | solution.py:109
  523.1 1.3 fusion.7
  524.4 69.9 %all-to-all-done.5 = f32[2,64,14,512]{3,0,2,1:T(2,128)} async-done(((f32[2,64,14,512]{3,0,2,1:T(2,128)}), f32[2,64,14,512]{3,0,2,1:T(2,128)}, u32[]{:S(2)}, u32[]{:S(2)}) %all-to-all-start.5) | async-done | bytes 3670048 | tf_op jit(solution)/shard_map/all_to_all | solution.py:38
  594.3 6.4 %fusion.22 = (f32[1,64,14,512]{3,0,2,1:T(1,128)S(1)}, f32[1,64,14,512]{3,0,2,1:T(1,128)S(1)}) fusion(f32[2,64,14,512]{3,0,2,1:T(2,128)} %all-to-all-done.5), kind=kLoop, calls=%fused_computation.64 | loop fusion | bytes 7340032 | tf_op jit(solution)/shard_map/slice | solution.py:119
  600.7 1.4 copy.45
  602.1 1.4 copy.46
  603.4 0.1 copy-done.1
  (37 shorter events, 0.3 us)
Async XLA Ops:
  7.2 1.2 copy-start
  7.2 51.4 %reduce-scatter.2.cloned.1.call-start = ((), (), s32[]{:S(2)}) async-start(), calls=%async_computation.7 | async-start | bytes 4587520 | tf_op jit(solution)/shard_map/reduce_scatter | solution.py:86
  12.2 0.8 copy-start.5
  12.2 1.2 copy-start.6
  12.2 46.4 %copy-start.3 = (f32[1,896,512]{2,1,0:T(8,128)S(1)}, f32[1,896,512]{2,1,0:T(8,128)}, u32[]{:S(2)}) copy-start(f32[1,896,512]{2,1,0:T(8,128)} %param.16) | copy-start | bytes 5505028
  64.1 14.1 %copy-start.7 = (s32[16]{0:T(128)S(1)}, s32[16]{0:T(128)}, u32[]{:S(2)}) copy-start(s32[16]{0:T(128)} %param.23) | copy-start | bytes 196
  65.3 15.2 %copy-start.2 = (s32[16]{0:T(128)S(1)}, s32[16]{0:T(128)}, u32[]{:S(2)}) copy-start(s32[16]{0:T(128)} %param.22) | copy-start | bytes 196
  65.3 43.3 %all-to-all-start.1 = ((bf16[64,14,512]{2,1,0:T(8,128)(2,1)}), bf16[64,14,512]{2,1,0:T(8,128)(2,1)S(1)}, u32[]{:S(2)}, u32[]{:S(2)}) async-start(bf16[64,14,512]{2,1,0:T(8,128)(2,1)} %reshape.97), calls=%async_computation.2 | async-start | bytes 2097152 | tf_op jit(solution)/shard_map/all_to_all | solution.py:33
  108.6 16.9 %all-to-all-start.3 = ((bf16[64,1,24]{2,1,0:T(2,128)(2,1)}), bf16[64,1,24]{2,1,0:T(2,128)(2,1)S(1)}, u32[]{:S(2)}, u32[]{:S(2)}) async-start(bf16[64,1,24]{2,1,0:T(2,128)(2,1)} %copy.43), calls=%async_computation.4 | async-start | bytes 65536 | tf_op jit(solution)/shard_map/all_to_all | solution.py:105
  125.5 34.0 %all-to-all-start.2 = ((bf16[64,14,512]{2,1,0:T(8,128)(2,1)}), bf16[64,14,512]{2,1,0:T(8,128)(2,1)S(1)}, u32[]{:S(2)}, u32[]{:S(2)}) async-start(bf16[64,14,512]{2,1,0:T(8,128)(2,1)} %broadcast_select_fusion.1), calls=%async_computation.3 | async-start | bytes 2097152 | tf_op jit(solution)/shard_map/all_to_all | solution.py:37
  144.3 21.6 %copy-start.4 = (bf16[1,1,128,3584]{3,2,1,0:T(8,128)(2,1)S(1)}, bf16[1,1,128,3584]{3,2,1,0:T(8,128)(2,1)}, u32[]{:S(2)}) copy-start(bf16[1,1,128,3584]{3,2,1,0:T(8,128)(2,1)} %param.18) | copy-start | bytes 2752516
  159.5 90.0 %all-to-all-start.4 = ((f32[2,64,14,512]{3,0,2,1:T(2,128)}), f32[2,64,14,512]{3,0,2,1:T(2,128)}, u32[]{:S(2)}, u32[]{:S(2)}) async-start(f32[2,64,14,512]{3,0,2,1:T(2,128)} %copy.44), calls=%async_computation.5 | async-start | bytes 7340032 | tf_op jit(solution)/shard_map/all_to_all | solution.py:34
  256.1 246.9 %all-to-all-start = ((bf16[64,24,3584]{2,1,0:T(8,128)(2,1)}), bf16[64,24,3584]{2,1,0:T(8,128)(2,1)}, u32[]{:S(2)}, u32[]{:S(2)}) async-start(bf16[64,24,3584]{2,1,0:T(8,128)(2,1)} %bitcast.52), calls=%async_computation | async-start | bytes 22020096 | tf_op jit(solution)/shard_map/all_to_all | solution.py:104
  263.2 250.2 %all-gather.2.cloned.1.call-start = ((), (), s32[]{:S(2)}) async-start(), calls=%async_computation.8 | async-start | bytes 4587520 | tf_op jit(solution)/shard_map/all_gather | solution.py:111
  502.9 91.4 %all-to-all-start.5 = ((f32[2,64,14,512]{3,0,2,1:T(2,128)}), f32[2,64,14,512]{3,0,2,1:T(2,128)}, u32[]{:S(2)}, u32[]{:S(2)}) async-start(f32[2,64,14,512]{3,0,2,1:T(2,128)} %select_bitcast_fusion), calls=%async_computation.6 | async-start | bytes 7340032 | tf_op jit(solution)/shard_map/all_to_all | solution.py:38
  602.1 1.5 copy-start.1
Sparse Core Ops, SparseCore 0:
  12.3 46.2 reduce-scatter.1
  266.4 78.0 all-gather.1
where the time goes:
time: 611 us; the launch traced here: 610 us
  waiting for transfers between devices  465 us (76%)
  starting transfers between devices  47 us (8%)
  local copies, waits for them, and re-layouts  46.9 us (8%)
  other arithmetic  20.7 us (3%)
  matrix products  16.1 us (3%)
  between operations  15 us (2%)
    all_to_all x1, waiting for transfers between devices, local(): lax.all_to_all(full_send, 'expert', split_axis=0, concat_axis=0, tiled=True)  225 us
    all_to_all x1, waiting for transfers between devices, migrate(): lax.all_to_all(moment_split, 'expert', split_axis=1, concat_axis=1, tiled...  73.4 us
    all_to_all x1, waiting for transfers between devices, migrate(): lax.all_to_all(moment_sorted, 'expert', split_axis=1, concat_axis=1, tile...  69.9 us
    reduce_scatter x1, waiting for transfers between devices, local(): lax.psum_scatter(lax.dot_general(columns, cotangent, (((0,), (0,)), ((),...  45.2 us
    all_to_all x1, waiting for transfers between devices, migrate(): lax.all_to_all(weight_split, 'expert', split_axis=0, concat_axis=0, tiled...  27.3 us
    all_to_all x1, waiting for transfers between devices, migrate(): lax.all_to_all(weight_sorted, 'expert', split_axis=0, concat_axis=0, tile...  15.2 us
    all_to_all x1, starting transfers between devices, migrate(): lax.all_to_all(weight_split, 'expert', split_axis=0, concat_axis=0, tiled...  12.7 us
  transfers between devices with their start and end apart: 8, of which 7 were waited for; matrix products, arithmetic and copies ran while one was open for 9% of the time, Pallas kernels for 0%

commit v1 on v0

--- a/solution.py
+++ b/solution.py
@@ -35,7 +35,12 @@
     weight_sorted = jnp.take(weight_spread, source, axis=0)
     moment_sorted = jnp.take(moment_spread, source, axis=1)
     weight_home = lax.all_to_all(weight_sorted, "expert", split_axis=0, concat_axis=0, tiled=True)
-    moment_home = lax.all_to_all(moment_sorted, "expert", split_axis=1, concat_axis=1, tiled=True)
+    moment_home = jnp.concatenate(
+        lax.all_to_all(
+            jnp.stack(jnp.split(moment_sorted, lax.axis_size("expert"), axis=1)), "expert", 0, 0
+        ),
+        axis=1,
+    )
     return (weight_home.reshape(rows_dev, width), moment_home.reshape(layers, rows_dev, width))
 
 

time: 611 us -> 611 us (level)
  local copies, waits for them, and re-layouts: 46.9 us -> 86.6 us
  waiting for transfers between devices: 465 us -> 427 us
    unnamed x18 -> x81, local copies, waits for them, and re-layouts: 3.99 us -> 43.1 us
    all_to_all x1, waiting for transfers between devices: 225 us -> 187 us  [local(): lax.all_to_all(full_send, 'expert', split_axis=0, concat_axis=0, tiled=True)]
  transfers between devices with their start and end apart: 8 -> 8, of which waited for: 7 -> 7; matrix products, arithmetic and copies ran while one was open for 9% -> 15% of each run, Pallas kernels for 0% -> 0%
where the time goes in v1:
time: 611 us; the launch traced here: 610 us
  waiting for transfers between devices  427 us (70%)
  local copies, waits for them, and re-layouts  86.6 us (14%)
  starting transfers between devices  46.9 us (8%)
  other arithmetic  19.1 us (3%)
  matrix products  16.1 us (3%)
  between operations  15 us (2%)
    all_to_all x1, waiting for transfers between devices, local(): lax.all_to_all(full_send, 'expert', split_axis=0, concat_axis=0, tiled=True)  187 us
    all_to_all x1, waiting for transfers between devices, migrate(): lax.all_to_all(moment_split, 'expert', split_axis=1, concat_axis=1, tiled...  73.5 us
    all_to_all x1, waiting for transfers between devices, migrate(): lax.all_to_all(jnp.stack(jnp.split(moment_sorted, lax.axis_size('expert')...  69.9 us
    reduce_scatter x1, waiting for transfers between devices, local(): lax.psum_scatter(lax.dot_general(columns, cotangent, (((0,), (0,)), ((),...  45.2 us
    unnamed x81, local copies, waits for them, and re-layouts  43.1 us
    all_to_all x1, waiting for transfers between devices, migrate(): lax.all_to_all(weight_split, 'expert', split_axis=0, concat_axis=0, tiled...  27.3 us
    all_to_all x1, waiting for transfers between devices, migrate(): lax.all_to_all(weight_sorted, 'expert', split_axis=0, concat_axis=0, tile...  15.2 us
    all_to_all x1, starting transfers between devices, migrate(): lax.all_to_all(weight_split, 'expert', split_axis=0, concat_axis=0, tiled...  12.6 us
  transfers between devices with their start and end apart: 8, of which 7 were waited for; matrix products, arithmetic and copies ran while one was open for 15% of the time, Pallas kernels for 0%

profile of v1, /device:TPU:32, one launch (start us, length us, event | category | flops | bytes accessed | tf_op | source)
XLA Modules:
  0.0 610.4 jit_solution(9138491471409374206)
XLA Ops:
  7.2 1.1 copy-done
  8.4 3.8 convolution_convert_fusion
  13.4 45.2 %reduce-scatter.2.cloned.1.call-done = bf16[896,512]{1,0:T(8,128)(2,1)} async-done(((bf16[3584,512]{1,0:T(8,128)(2,1)}), bf16[896,512]{1,0:T(8,128)(2,1)}) %reduce-scatter.2.cloned.1.call-update) | async-done | bytes 917520 | tf_op jit(solution)/shard_map/reduce_scatter | solution.py:91
  58.6 5.7 fusion.2
  64.3 1.2 reshape.99
  65.5 12.6 %all-to-all-start.1 = ((bf16[64,14,512]{2,1,0:T(8,128)(2,1)}), bf16[64,14,512]{2,1,0:T(8,128)(2,1)S(1)}, u32[]{:S(2)}, u32[]{:S(2)}) async-start(bf16[64,14,512]{2,1,0:T(8,128)(2,1)} %reshape.99), calls=%async_computation.2 | async-start | bytes 2097152 | tf_op jit(solution)/shard_map/all_to_all | solution.py:33
  78.5 0.8 gather_fusion.4
  79.9 0.6 copy.43
  80.6 0.8 gather_fusion.5
  81.4 27.3 %all-to-all-done.1 = bf16[64,14,512]{2,1,0:T(8,128)(2,1)S(1)} async-done(((bf16[64,14,512]{2,1,0:T(8,128)(2,1)}), bf16[64,14,512]{2,1,0:T(8,128)(2,1)S(1)}, u32[]{:S(2)}, u32[]{:S(2)}) %all-to-all-start.1) | async-done | bytes 917536 | tf_op jit(solution)/shard_map/all_to_all | solution.py:33
  108.7 6.0 all-to-all-start.3
  115.3 1.1 broadcast_select_fusion.1
  116.4 9.2 %all-to-all-done.3 = bf16[64,1,24]{2,1,0:T(2,128)(2,1)S(1)} async-done(((bf16[64,1,24]{2,1,0:T(2,128)(2,1)}), bf16[64,1,24]{2,1,0:T(2,128)(2,1)S(1)}, u32[]{:S(2)}, u32[]{:S(2)}) %all-to-all-start.3) | async-done | bytes 3104 | tf_op jit(solution)/shard_map/all_to_all | solution.py:110
  125.6 5.6 all-to-all-start.2
  131.2 2.7 stack.205
  133.9 2.7 stack.204
  136.5 2.7 pad_maximum_fusion
  139.3 5.1 copy.44
  144.4 15.2 %all-to-all-done.2 = bf16[64,14,512]{2,1,0:T(8,128)(2,1)S(1)} async-done(((bf16[64,14,512]{2,1,0:T(8,128)(2,1)}), bf16[64,14,512]{2,1,0:T(8,128)(2,1)S(1)}, u32[]{:S(2)}, u32[]{:S(2)}) %all-to-all-start.2) | async-done | bytes 917536 | tf_op jit(solution)/shard_map/all_to_all | solution.py:37
  159.6 6.4 %all-to-all-start.4 = ((f32[2,64,14,512]{3,0,2,1:T(2,128)}), f32[2,64,14,512]{3,0,2,1:T(2,128)}, u32[]{:S(2)}, u32[]{:S(2)}) async-start(f32[2,64,14,512]{3,0,2,1:T(2,128)} %copy.44), calls=%async_computation.5 | async-start | bytes 7340032 | tf_op jit(solution)/shard_map/all_to_all | solution.py:34
  166.1 2.4 convolution_convert_fusion.1
  168.5 4.0 gather_fusion
  172.5 3.6 broadcast_select_fusion
  176.1 73.5 %all-to-all-done.4 = f32[2,64,14,512]{3,0,2,1:T(2,128)} async-done(((f32[2,64,14,512]{3,0,2,1:T(2,128)}), f32[2,64,14,512]{3,0,2,1:T(2,128)}, u32[]{:S(2)}, u32[]{:S(2)}) %all-to-all-start.4) | async-done | bytes 3670048 | tf_op jit(solution)/shard_map/all_to_all | solution.py:34
  249.6 6.6 %broadcast_in_dim.92 = bf16[16,4,24,3584]{3,2,1,0:T(8,128)(2,1)} broadcast(bf16[16,24,3584]{2,1,0:T(8,128)(2,1)} %broadcast_select_fusion), dimensions={0,2,3} | broadcast | bytes 13762560 | tf_op jit(solution)/shard_map/broadcast_in_dim | solution.py:107
  256.2 7.1 %all-to-all-start = ((bf16[64,24,3584]{2,1,0:T(8,128)(2,1)}), bf16[64,24,3584]{2,1,0:T(8,128)(2,1)}, u32[]{:S(2)}, u32[]{:S(2)}) async-start(bf16[64,24,3584]{2,1,0:T(8,128)(2,1)} %bitcast.309), calls=%async_computation | async-start | bytes 22020096 | tf_op jit(solution)/shard_map/all_to_all | solution.py:109
  263.3 1.2 reshape.100
  264.6 8.1 %gather_fusion.3 = f32[64,2,14,512]{3,1,2,0:T(2,128)} fusion(f32[2,64,14,512]{3,0,2,1:T(2,128)} %all-to-all-done.4, s32[1024]{0:T(1024)S(1)} %pad_clamp_fusion), kind=kCustom, calls=%fused_computation.5 | custom fusion | bytes 7340288 | tf_op jit(solution)/shard_map/jit(_take)/gather | solution.py:36
  272.6 4.0 select_bitcast_fusion
  279.1 0.6 constant_dynamic-update-slice_fusion.59
  281.0 0.6 constant_dynamic-update-slice_fusion.56
  284.1 0.6 constant_dynamic-update-slice_fusion.51
  288.5 0.6 constant_dynamic-update-slice_fusion.44
  289.1 0.6 constant_dynamic-update-slice_fusion.43
  294.1 0.6 constant_dynamic-update-slice_fusion.35
  297.8 0.6 constant_dynamic-update-slice_fusion.29
  301.5 0.6 constant_dynamic-update-slice_fusion.23
  306.5 0.6 constant_dynamic-update-slice_fusion.15
  313.4 0.6 constant_dynamic-update-slice_fusion.4
  316.5 186.6 %all-to-all-done = bf16[64,24,3584]{2,1,0:T(8,128)(2,1)} async-done(((bf16[64,24,3584]{2,1,0:T(8,128)(2,1)}), bf16[64,24,3584]{2,1,0:T(8,128)(2,1)}, u32[]{:S(2)}, u32[]{:S(2)}) %all-to-all-start) | async-done | bytes 11010080 | tf_op jit(solution)/shard_map/all_to_all | solution.py:109
  503.1 9.1 %all-to-all-start.5 = ((f32[64,2,1,14,512]{4,1,3,2,0:T(2,128)}), f32[64,2,1,14,512]{4,1,3,2,0:T(2,128)}, u32[]{:S(2)}, u32[]{:S(2)}) async-start(f32[64,2,1,14,512]{4,1,3,2,0:T(2,128)} %constant_dynamic-update-slice_fusion), calls=%async_computation.6 | async-start | bytes 7340032 | tf_op jit(solution)/shard_map/all_to_all | solution.py:39
  512.4 1.2 broadcast_in_dim_reshape.3
  513.5 9.7 %fusion.23 = f32[1536,512]{1,0:T(8,128)S(1)} fusion(bf16[1536,3584]{1,0:T(8,128)(2,1)} %bitcast.9, bf16[3584,512]{1,0:T(8,128)(2,1)} %all-gather.2.cloned.1.call-done), kind=kOutput, calls=%fused_computation.193 | convolution fusion | flops 5637144576 | bytes 17825792 | tf_op jit(solution)/shard_map/dot_general | solution.py:114
  523.2 1.3 fusion.7
  524.6 69.9 %all-to-all-done.5 = f32[64,2,1,14,512]{4,1,3,2,0:T(2,128)} async-done(((f32[64,2,1,14,512]{4,1,3,2,0:T(2,128)}), f32[64,2,1,14,512]{4,1,3,2,0:T(2,128)}, u32[]{:S(2)}, u32[]{:S(2)}) %all-to-all-start.5) | async-done | bytes 3670048 | tf_op jit(solution)/shard_map/all_to_all | solution.py:39
  594.4 6.4 %fusion.22 = (f32[1,64,1,14,512]{4,0,3,2,1:T(1,128)S(1)}, f32[1,64,1,14,512]{4,0,3,2,1:T(1,128)S(1)}) fusion(f32[2,64,1,14,512]{4,0,3,2,1:T(2,128)} %bitcast.87), kind=kLoop, calls=%fused_computation.192 | loop fusion | bytes 7340032 | tf_op jit(solution)/shard_map/slice | solution.py:124
  600.8 1.4 copy.45
  602.2 1.4 copy.46
  (100 shorter events, 35.8 us)
Async XLA Ops:
  7.2 1.2 copy-start
  7.2 51.4 %reduce-scatter.2.cloned.1.call-start = ((), (), s32[]{:S(2)}) async-start(), calls=%async_computation.7 | async-start | bytes 4587520 | tf_op jit(solution)/shard_map/reduce_scatter | solution.py:91
  12.2 0.8 copy-start.5
  12.2 1.1 copy-start.6
  12.2 46.4 %copy-start.3 = (bf16[1,896,512]{2,1,0:T(8,128)(2,1)S(1)}, bf16[1,896,512]{2,1,0:T(8,128)(2,1)}, u32[]{:S(2)}) copy-start(bf16[1,896,512]{2,1,0:T(8,128)(2,1)} %param.15) | copy-start | bytes 2752516
  64.3 14.0 %copy-start.7 = (s32[16]{0:T(128)S(1)}, s32[16]{0:T(128)}, u32[]{:S(2)}) copy-start(s32[16]{0:T(128)} %param.23) | copy-start | bytes 196
  64.3 16.3 %copy-start.2 = (s32[16]{0:T(128)S(1)}, s32[16]{0:T(128)}, u32[]{:S(2)}) copy-start(s32[16]{0:T(128)} %param.22) | copy-start | bytes 196
  65.5 43.1 %all-to-all-start.1 = ((bf16[64,14,512]{2,1,0:T(8,128)(2,1)}), bf16[64,14,512]{2,1,0:T(8,128)(2,1)S(1)}, u32[]{:S(2)}, u32[]{:S(2)}) async-start(bf16[64,14,512]{2,1,0:T(8,128)(2,1)} %reshape.99), calls=%async_computation.2 | async-start | bytes 2097152 | tf_op jit(solution)/shard_map/all_to_all | solution.py:33
  108.7 16.9 %all-to-all-start.3 = ((bf16[64,1,24]{2,1,0:T(2,128)(2,1)}), bf16[64,1,24]{2,1,0:T(2,128)(2,1)S(1)}, u32[]{:S(2)}, u32[]{:S(2)}) async-start(bf16[64,1,24]{2,1,0:T(2,128)(2,1)} %copy.43), calls=%async_computation.4 | async-start | bytes 65536 | tf_op jit(solution)/shard_map/all_to_all | solution.py:110
  125.6 34.0 %all-to-all-start.2 = ((bf16[64,14,512]{2,1,0:T(8,128)(2,1)}), bf16[64,14,512]{2,1,0:T(8,128)(2,1)S(1)}, u32[]{:S(2)}, u32[]{:S(2)}) async-start(bf16[64,14,512]{2,1,0:T(8,128)(2,1)} %broadcast_select_fusion.1), calls=%async_computation.3 | async-start | bytes 2097152 | tf_op jit(solution)/shard_map/all_to_all | solution.py:37
  144.4 21.7 %copy-start.4 = (bf16[1,1,128,3584]{3,2,1,0:T(8,128)(2,1)S(1)}, bf16[1,1,128,3584]{3,2,1,0:T(8,128)(2,1)}, u32[]{:S(2)}) copy-start(bf16[1,1,128,3584]{3,2,1,0:T(8,128)(2,1)} %param.18) | copy-start | bytes 2752516
  159.6 90.0 %all-to-all-start.4 = ((f32[2,64,14,512]{3,0,2,1:T(2,128)}), f32[2,64,14,512]{3,0,2,1:T(2,128)}, u32[]{:S(2)}, u32[]{:S(2)}) async-start(f32[2,64,14,512]{3,0,2,1:T(2,128)} %copy.44), calls=%async_computation.5 | async-start | bytes 7340032 | tf_op jit(solution)/shard_map/all_to_all | solution.py:34
  256.2 246.9 %all-to-all-start = ((bf16[64,24,3584]{2,1,0:T(8,128)(2,1)}), bf16[64,24,3584]{2,1,0:T(8,128)(2,1)}, u32[]{:S(2)}, u32[]{:S(2)}) async-start(bf16[64,24,3584]{2,1,0:T(8,128)(2,1)} %bitcast.309), calls=%async_computation | async-start | bytes 22020096 | tf_op jit(solution)/shard_map/all_to_all | solution.py:109
  263.3 250.2 %all-gather.2.cloned.1.call-start = ((), (), s32[]{:S(2)}) async-start(), calls=%async_computation.8 | async-start | bytes 4587520 | tf_op jit(solution)/shard_map/all_gather | solution.py:116
  503.1 91.4 %all-to-all-start.5 = ((f32[64,2,1,14,512]{4,1,3,2,0:T(2,128)}), f32[64,2,1,14,512]{4,1,3,2,0:T(2,128)}, u32[]{:S(2)}, u32[]{:S(2)}) async-start(f32[64,2,1,14,512]{4,1,3,2,0:T(2,128)} %constant_dynamic-update-slice_fusion), calls=%async_computation.6 | async-start | bytes 7340032 | tf_op jit(solution)/shard_map/all_to_all | solution.py:39
  600.8 2.8 copy-start.1
Sparse Core Ops, SparseCore 0:
  12.3 46.2 reduce-scatter.1
  266.5 78.0 all-gather.1
